TPU v7x, 32 devices: a whole 2x2x4 slice. The times are simulated.
32 devices in a mesh: dp: 8 (over y, x, core), fsdp: 4 (over z).
Axes of the slice: x: 2, y: 2, z: 4, core: 2. Of those that a mesh axis runs over, the one named last changes fastest.
Arguments:
- tokens: bfloat16 [18432, 768], P(('dp', 'fsdp')), may hold values from -6 to 6
- image_lengths: int32 [32, 9], P(('dp', 'fsdp')), may hold values from 0 to 576, as said below
- w_qkv: bfloat16 [768, 2304], P('fsdp'), may hold values from -0.21875 to 0.21875
- w_out: bfloat16 [768, 768], P('fsdp'), may hold values from -0.875 to 0.875
- w_up: bfloat16 [768, 3072], P('fsdp'), may hold values from -0.21875 to 0.21875
- w_down: bfloat16 [3072, 768], P('fsdp'), may hold values from -0.109375 to 0.109375
- ln_gain: bfloat16 [2, 768], P(None, 'fsdp'), may hold values from 0.25 to 1.75
- ln_bias: bfloat16 [2, 768], P(None, 'fsdp'), may hold values from -3 to 3
- qk_gain: bfloat16 [2, 768], P(None, 'fsdp'), may hold values from 0.25 to 1.75
- cotangent: bfloat16 [18432, 768], P(('dp', 'fsdp')), may hold values from -6 to 6
Outputs:
- layer_out: bfloat16 [18432, 768], P(('dp', 'fsdp'))
- grad_tokens: bfloat16 [18432, 768], P(('dp', 'fsdp'))
- grad_w_qkv: float32 [768, 2304], P('fsdp')
- grad_w_out: float32 [768, 768], P('fsdp')
- grad_w_up: float32 [768, 3072], P('fsdp')
- grad_w_down: float32 [3072, 768], P('fsdp')
- grad_ln_gain: float32 [2, 768], P(None, 'fsdp')
- grad_ln_bias: float32 [2, 768], P(None, 'fsdp')
- grad_qk_gain: float32 [2, 768], P(None, 'fsdp')
Inputs may be any that keep to these rules, and one draw needn't show every extreme that they name: Each row of image_lengths is either 1 large images of 576 patches, or between 1 and 9 small images of 64 patches; used slots come first, zeros after. Exactly half of the rows hold large images. No image crosses a multiple of 576 rows, and padding lies after the last image.
All inputs are finite; a program needn't handle non-finite values.
Results may differ from a plain program's by a relative error of at most 0.02.
Values may be sent and summed in bfloat16 or wider, within the bound.
No kernel may reach another device: no remote copies, remote signals or barrier semaphores. Data moves between devices by JAX's collectives and lax.ppermute only.
A program may use at most 192 MiB of HBM per device.

v0:
```python
from functools import partial
import jax
import jax.numpy as jnp
from jax import lax
from jax.sharding import PartitionSpec as P

HEADS = 12
HEAD_DIM = 64
PATCH_BIG = 576
epsilon = 1e-06


def layer_norm(v, gain_row, bias_row):
    centre = v - jnp.mean(v, axis=-1, keepdims=True)
    spread = jnp.mean(centre * centre, axis=-1, keepdims=True)
    return centre * lax.rsqrt(spread + epsilon) * gain_row + bias_row


def head_norm(v, gain_row):
    centre = v - jnp.mean(v, axis=-1, keepdims=True)
    spread = jnp.mean(centre * centre, axis=-1, keepdims=True)
    return centre * lax.rsqrt(spread + epsilon) * gain_row


def both_norms(q_in, k_in, q_gain, k_gain):
    return (head_norm(q_in, q_gain), head_norm(k_in, k_gain))


def on_device(
    tokens, image_lengths, w_qkv, w_out, w_up, w_down, ln_gain, ln_bias, qk_gain, cotangent
):
    full_qkv, full_out, full_up, full_down, gain_all, bias_all, qk_all = (
        lax.all_gather(w_qkv, "fsdp", axis=0, tiled=True),
        lax.all_gather(w_out, "fsdp", axis=0, tiled=True),
        lax.all_gather(w_up, "fsdp", axis=0, tiled=True),
        lax.all_gather(w_down, "fsdp", axis=0, tiled=True),
        lax.all_gather(ln_gain, "fsdp", axis=1, tiled=True),
        lax.all_gather(ln_bias, "fsdp", axis=1, tiled=True),
        lax.all_gather(qk_gain, "fsdp", axis=1, tiled=True),
    )
    length = tokens.shape[0]
    model_width = tokens.shape[1]
    blocks = length // PATCH_BIG
    scaling = HEAD_DIM ** (-0.5)
    position = jnp.arange(length, dtype=jnp.int32)
    limits = jnp.cumsum(image_lengths[0])
    segment = jnp.sum((position[:, None] >= limits[None, :]).astype(jnp.int32), axis=1)
    valid_rows = (position < limits[-1]).astype(jnp.float32)[:, None]
    norm_gains = gain_all.astype(jnp.float32)
    biases = bias_all.astype(jnp.float32)
    qk_gains = qk_all.astype(jnp.float32).reshape(2, HEADS, HEAD_DIM)
    inputs = tokens.astype(jnp.float32)
    normed, first_back = jax.vjp(layer_norm, inputs, norm_gains[0], biases[0])
    normed_low = normed.astype(jnp.bfloat16)
    project = jnp.dot(normed_low, full_qkv, preferred_element_type=jnp.float32)
    queries = project[:, :model_width].reshape(length, HEADS, HEAD_DIM)
    keys_raw = project[:, model_width : 2 * model_width].reshape(length, HEADS, HEAD_DIM)
    values_raw = project[:, 2 * model_width :]
    (q_norm, k_norm), norms_back = jax.vjp(both_norms, queries, keys_raw, qk_gains[0], qk_gains[1])
    q_low = q_norm.astype(jnp.bfloat16).reshape(blocks, PATCH_BIG, HEADS, HEAD_DIM)
    k_low = k_norm.astype(jnp.bfloat16).reshape(blocks, PATCH_BIG, HEADS, HEAD_DIM)
    v_low = values_raw.astype(jnp.bfloat16).reshape(blocks, PATCH_BIG, HEADS, HEAD_DIM)
    s_blocks = segment.reshape(blocks, PATCH_BIG)

    def block_scores(q_block, k_block, s_block):
        scores = (
            jnp.einsum("qhd,khd->hqk", q_block, k_block, preferred_element_type=jnp.float32)
            * scaling
        )
        return jnp.where((s_block[:, None] == s_block[None, :])[None], scores, -1e30)

    def attend(members):
        q_block, k_block, v_block, s_block = members
        scores = block_scores(q_block, k_block, s_block)
        row_top = jnp.max(scores, axis=-1, keepdims=True)
        exp_scores = jnp.exp(scores - row_top)
        row_total = jnp.sum(exp_scores, axis=-1, keepdims=True)
        probability = (exp_scores / row_total).astype(jnp.bfloat16)
        mixed_block = jnp.einsum(
            "hqk,khd->qhd", probability, v_block, preferred_element_type=jnp.float32
        )
        return (mixed_block, row_top + jnp.log(row_total))

    mixed_heads, log_total = lax.map(attend, (q_low, k_low, v_low, s_blocks))
    mixed_low = mixed_heads.reshape(length, model_width).astype(jnp.bfloat16)
    residual = inputs + jnp.dot(mixed_low, full_out, preferred_element_type=jnp.float32)
    second, second_back = jax.vjp(layer_norm, residual, norm_gains[1], biases[1])
    second_low = second.astype(jnp.bfloat16)
    up_pre = jnp.dot(second_low, full_up, preferred_element_type=jnp.float32)
    active, gelu_back = jax.vjp(partial(jax.nn.gelu, approximate=False), up_pre)
    active_low = active.astype(jnp.bfloat16)
    output = residual + jnp.dot(active_low, full_down, preferred_element_type=jnp.float32)
    layer_out = (valid_rows * output).astype(jnp.bfloat16)
    back_qkv, back_out, back_up, back_down = (
        lax.all_gather(w_qkv, "fsdp", axis=0, tiled=True),
        lax.all_gather(w_out, "fsdp", axis=0, tiled=True),
        lax.all_gather(w_up, "fsdp", axis=0, tiled=True),
        lax.all_gather(w_down, "fsdp", axis=0, tiled=True),
    )
    upstream = cotangent.astype(jnp.float32) * valid_rows
    up_low = upstream.astype(jnp.bfloat16)
    grad_down = jnp.dot(active_low.T, up_low, preferred_element_type=jnp.float32)
    grad_active = jnp.dot(up_low, back_down.T, preferred_element_type=jnp.float32)
    (grad_pre,) = gelu_back(grad_active)
    pre_low = grad_pre.astype(jnp.bfloat16)
    grad_up = jnp.dot(second_low.T, pre_low, preferred_element_type=jnp.float32)
    grad_second = jnp.dot(pre_low, back_up.T, preferred_element_type=jnp.float32)
    grad_resid, gain_two, bias_two = second_back(grad_second)
    grad_resid = grad_resid + upstream
    resid_low = grad_resid.astype(jnp.bfloat16)
    grad_outw = jnp.dot(mixed_low.T, resid_low, preferred_element_type=jnp.float32)
    grad_mixed = jnp.dot(resid_low, back_out.T, preferred_element_type=jnp.float32)
    grad_mixed = grad_mixed.astype(jnp.bfloat16).reshape(blocks, PATCH_BIG, HEADS, HEAD_DIM)

    def attend_back(members):
        q_block, k_block, v_block, s_block, l_block, d_block = members
        scores = block_scores(q_block, k_block, s_block)
        probability = jnp.exp(scores - l_block)
        prob_low = probability.astype(jnp.bfloat16)
        grad_v = jnp.einsum("hqk,qhd->khd", prob_low, d_block, preferred_element_type=jnp.float32)
        grad_p = jnp.einsum("qhd,khd->hqk", d_block, v_block, preferred_element_type=jnp.float32)
        grad_p = lax.optimization_barrier(grad_p.astype(jnp.bfloat16)).astype(jnp.float32)
        grad_s = probability * (grad_p - jnp.sum(probability * grad_p, axis=-1, keepdims=True))
        s_low = grad_s.astype(jnp.bfloat16)
        grad_q = (
            jnp.einsum("hqk,khd->qhd", s_low, k_block, preferred_element_type=jnp.float32) * scaling
        )
        grad_k = (
            jnp.einsum("hqk,qhd->khd", s_low, q_block, preferred_element_type=jnp.float32) * scaling
        )
        return (grad_q, grad_k, grad_v)

    grad_qn, grad_kn, grad_vn = lax.map(
        attend_back, (q_low, k_low, v_low, s_blocks, log_total, grad_mixed)
    )
    grad_q, grad_k, gain_q, gain_k = norms_back(
        (grad_qn.reshape(length, HEADS, HEAD_DIM), grad_kn.reshape(length, HEADS, HEAD_DIM))
    )
    grad_project = jnp.concatenate(
        [
            grad_q.reshape(length, model_width),
            grad_k.reshape(length, model_width),
            grad_vn.reshape(length, model_width),
        ],
        axis=1,
    ).astype(jnp.bfloat16)
    grad_qkv = jnp.dot(normed_low.T, grad_project, preferred_element_type=jnp.float32)
    grad_normed = jnp.dot(grad_project, back_qkv.T, preferred_element_type=jnp.float32)
    grad_input, gain_one, bias_one = first_back(grad_normed)
    grad_tokens = (grad_input + grad_resid).astype(jnp.bfloat16)
    grad_gain = jnp.stack([gain_one, gain_two])
    grad_bias = jnp.stack([bias_one, bias_two])
    grad_qk = jnp.stack([gain_q.reshape(model_width), gain_k.reshape(model_width)])
    summands = (grad_qkv, grad_outw, grad_up, grad_down, grad_gain, grad_bias, grad_qk)
    pieces = (
        lax.psum_scatter(
            summands[0].astype(jnp.bfloat16), "fsdp", scatter_dimension=0, tiled=True
        ).astype(jnp.float32),
        lax.psum_scatter(
            summands[1].astype(jnp.bfloat16), "fsdp", scatter_dimension=0, tiled=True
        ).astype(jnp.float32),
        lax.psum_scatter(
            summands[2].astype(jnp.bfloat16), "fsdp", scatter_dimension=0, tiled=True
        ).astype(jnp.float32),
        lax.psum_scatter(
            summands[3].astype(jnp.bfloat16), "fsdp", scatter_dimension=0, tiled=True
        ).astype(jnp.float32),
        lax.psum_scatter(
            summands[4].astype(jnp.bfloat16), "fsdp", scatter_dimension=1, tiled=True
        ).astype(jnp.float32),
        lax.psum_scatter(
            summands[5].astype(jnp.bfloat16), "fsdp", scatter_dimension=1, tiled=True
        ).astype(jnp.float32),
        lax.psum_scatter(
            summands[6].astype(jnp.bfloat16), "fsdp", scatter_dimension=1, tiled=True
        ).astype(jnp.float32),
    )
    shares = (
        lax.psum(pieces[0].astype(jnp.bfloat16), "dp").astype(jnp.float32),
        lax.psum(pieces[1].astype(jnp.bfloat16), "dp").astype(jnp.float32),
        lax.psum(pieces[2].astype(jnp.bfloat16), "dp").astype(jnp.float32),
        lax.psum(pieces[3].astype(jnp.bfloat16), "dp").astype(jnp.float32),
        lax.psum(pieces[4].astype(jnp.bfloat16), "dp").astype(jnp.float32),
        lax.psum(pieces[5].astype(jnp.bfloat16), "dp").astype(jnp.float32),
        lax.psum(pieces[6].astype(jnp.bfloat16), "dp").astype(jnp.float32),
    )
    return (
        layer_out,
        grad_tokens,
        shares[0],
        shares[1],
        shares[2],
        shares[3],
        shares[4],
        shares[5],
        shares[6],
    )


def solution(mesh):
    in_specs = (
        P(("dp", "fsdp"), None),
        P(("dp", "fsdp"), None),
        P("fsdp", None),
        P("fsdp", None),
        P("fsdp", None),
        P("fsdp", None),
        P(None, "fsdp"),
        P(None, "fsdp"),
        P(None, "fsdp"),
        P(("dp", "fsdp"), None),
    )
    out_specs = (
        P(("dp", "fsdp"), None),
        P(("dp", "fsdp"), None),
        P("fsdp", None),
        P("fsdp", None),
        P("fsdp", None),
        P("fsdp", None),
        P(None, "fsdp"),
        P(None, "fsdp"),
        P(None, "fsdp"),
    )
    return jax.shard_map(
        on_device, mesh=mesh, in_specs=in_specs, out_specs=out_specs, check_vma=False
    )
```

profile of v0, /device:TPU:0, one launch (start us, length us, event | category | flops | bytes accessed | tf_op | source)
XLA Modules:
  0.0 768.0 jit_solution(16090609015939321576)
XLA Ops:
  11.6 12.7 %all-gather = bf16[4,192,2]{1,2,0:T(2,128)(2,1)S(1)} all-gather(bf16[1,192,2]{1,2,0:T(2,128)(2,1)S(1)} %bitcast.126), channel_id=1, replica_groups=mesh['dp'=8,'fsdp'=4] {'fsdp'}, dimensions={0}, use_global_device_ids=true | all-gather | bytes 3840 | tf_op jit(solution)/shard_map/all_gather | solution.py:37
  24.4 8.1 %all-gather.1 = bf16[4,192,2]{1,2,0:T(2,128)(2,1)S(1)} all-gather(bf16[1,192,2]{1,2,0:T(2,128)(2,1)S(1)} %bitcast.127), channel_id=1, replica_groups=mesh['dp'=8,'fsdp'=4] {'fsdp'}, dimensions={0}, use_global_device_ids=true | all-gather | bytes 3840 | tf_op jit(solution)/shard_map/all_gather | solution.py:38
  32.5 10.7 %all-gather.2 = bf16[4,192,2]{1,2,0:T(2,128)(2,1)S(1)} all-gather(bf16[1,192,2]{1,2,0:T(2,128)(2,1)S(1)} %bitcast.128), channel_id=1, replica_groups=mesh['dp'=8,'fsdp'=4] {'fsdp'}, dimensions={0}, use_global_device_ids=true | all-gather | bytes 3840 | tf_op jit(solution)/shard_map/all_gather | solution.py:39
  44.5 37.8 %all-gather.8.cloned.1.call-done = bf16[768,2304]{1,0:T(8,128)(2,1)} async-done(((bf16[192,2304]{1,0:T(8,128)(2,1)}), bf16[768,2304]{1,0:T(8,128)(2,1)}) %all-gather.8.cloned.1.call-update) | async-done | bytes 3538960 | tf_op jit(solution)/shard_map/all_gather | solution.py:33
  99.4 8.1 %fusion.62 = (f32[12,576]{1,0:T(8,128)S(1)}, f32[12,576,576]{1,2,0:T(8,128)}) fusion(f32[576,12,64]{0,2,1:T(8,128)S(1)} %bitcast.95, f32[12,64]{1,0:T(8,128)S(1)} %mul.324, f32[576,12]{0,1:T(8,128)S(1)} %fusion.47, f32[576,12]{0,1:T(8,128)S(1)} %broadcast_multiply_fusion, f32[576,12,64]{0,2,1:T(8,128)S(1)} %bitcast.102, f32[12,64]{1,0:T(8,128)S(1)} %mul.318, ...), kind=kOutput, calls=%fused_computation.139 | convolution fusion | flops 525083904 | bytes 19940352 | tf_op jit(solution)/shard_map/while/body/eval_jaxpr/qhd,khd->hqk/dot_general | solution.py:67
  107.5 8.5 %fusion.3 = f32[12,576]{1,0:T(8,128)S(1)} fusion(f32[12,576,576]{1,2,0:T(8,128)} %get-tuple-element.91, f32[12,576]{1,0:T(8,128)S(1)} %get-tuple-element.90), kind=kLoop, calls=%fused_computation.9 | loop fusion | flops 7955712 | bytes 15980544 | tf_op jit(solution)/shard_map/while/body/eval_jaxpr/reduce_sum | solution.py:77
  116.0 11.4 %fusion.31 = bf16[12,64,576]{2,1,0:T(8,128)(2,1)} fusion(bf16[576,12,64]{0,2,1:T(8,128)(2,1)} %bitcast.109, f32[12,576,576]{1,2,0:T(8,128)} %get-tuple-element.91, f32[12,576]{1,0:T(8,128)S(1)} %fusion.3, f32[12,576]{1,0:T(8,128)S(1)} %get-tuple-element.90), kind=kOutput, calls=%fused_computation.81 | convolution fusion | flops 521994240 | bytes 17750016 | tf_op jit(solution)/shard_map/while/body/eval_jaxpr/hqk,khd->qhd/dot_general | solution.py:79
  131.5 71.6 %all-gather.12.cloned.1.call-done = bf16[768,3072]{1,0:T(8,128)(2,1)} async-done(((bf16[192,3072]{1,0:T(8,128)(2,1)}), bf16[768,3072]{1,0:T(8,128)(2,1)}) %all-gather.12.cloned.1.call-update) | async-done | bytes 4718608 | tf_op jit(solution)/shard_map/all_gather | solution.py:35
  203.1 22.8 %multiply_convert_fusion = (bf16[576,3072]{1,0:T(8,128)(2,1)}, f32[576,3072]{1,0:T(8,128)}, f32[576,3072]{1,0:T(8,128)}) fusion(bf16[768,3072]{1,0:T(8,128)(2,1)} %all-gather.12.cloned.1.call-done, f32[576,768]{1,0:T(8,128)} %copy-done.7, f32[768]{0:T(1024)S(1)} %get-tuple-element.73, f32[768]{0:T(1024)S(1)} %get-tuple-element.102, f32[576]{0:T(1024)S(1)} %fusion.50, ...), kind=kOutput, calls=%fused_computation.17 | convolution fusion | flops 2835136512 | bytes 24193536 | tf_op jit(solution)/shard_map/dot_general | solution.py:89
  225.8 66.5 %all-gather.14.cloned.1.call-done = bf16[3072,768]{1,0:T(8,128)(2,1)} async-done(((bf16[768,768]{1,0:T(8,128)(2,1)}), bf16[3072,768]{1,0:T(8,128)(2,1)}) %all-gather.14.cloned.1.call-update) | async-done | bytes 4718608 | tf_op jit(solution)/shard_map/all_gather | solution.py:36
  292.4 11.3 %add_convert_fusion = bf16[576,3072]{1,0:T(8,128)(2,1)S(1)} fusion(f32[576,3072]{1,0:T(8,128)} %get-tuple-element.87, f32[576,3072]{1,0:T(8,128)} %get-tuple-element.94, bf16[3072,768]{1,0:T(8,128)(2,1)} %all-gather.14.cloned.1.call-done, bf16[576,768]{1,0:T(8,128)(2,1)} %param.19, f32[576]{0:T(1024)S(1)} %fusion.48), kind=kOutput, calls=%fused_computation.16 | convolution fusion | flops 2744008704 | bytes 23300352 | tf_op jit(solution)/shard_map/dot_general | solution.py:103
  318.2 7.6 convolution_convert_fusion
  325.8 12.0 %fusion = f32[12,576]{1,0:T(8,128)S(1)} fusion(bf16[12,576,576]{1,2,0:T(8,128)(2,1)} %convolution_convert_fusion, f32[12,576,576]{1,2,0:T(8,128)} %get-tuple-element.91, f32[12,576]{1,0:T(8,128)S(1)} %log_add_fusion), kind=kLoop, calls=%fused_computation.2 | loop fusion | flops 15918336 | bytes 23943168 | tf_op jit(solution)/shard_map/while/body/eval_jaxpr/reduce_sum | solution.py:123
  356.0 9.2 %fusion.32 = bf16[12,64,576]{2,1,0:T(8,128)(2,1)S(1)} fusion(bf16[576,12,64]{0,2,1:T(8,128)(2,1)S(1)} %bitcast.108, f32[12,576,576]{1,2,0:T(8,128)} %get-tuple-element.91, f32[12,576]{1,0:T(8,128)S(1)} %log_add_fusion), kind=kOutput, calls=%fused_computation.82 | convolution fusion | flops 518012928 | bytes 17722368 | tf_op jit(solution)/shard_map/while/body/eval_jaxpr/hqk,qhd->khd/dot_general | solution.py:120
  374.9 7.8 %convolution_convert_fusion.3 = bf16[768,3072]{1,0:T(8,128)(2,1)} fusion(bf16[576,3072]{1,0:T(8,128)(2,1)} %copy-done.38, f32[576,768]{1,0:T(8,128)S(1)} %copy-done.9, f32[768]{0:T(1024)S(1)} %get-tuple-element.73, f32[768]{0:T(1024)S(1)} %get-tuple-element.102, f32[576]{0:T(1024)S(1)} %fusion.50, f32[576]{0:T(1024)S(1)} %broadcast_multiply_fusion.4), kind=kOutput, calls=%fused_computation.34 | convolution fusion | flops 2722480128 | bytes 10037760 | tf_op jit(solution)/shard_map/dot_general | solution.py:106
  383.9 8.0 %convolution_convert_fusion.2 = bf16[3072,768]{1,0:T(8,128)(2,1)} fusion(bf16[576,3072]{1,0:T(8,128)(2,1)} %get-tuple-element.86, bf16[576,768]{1,0:T(8,128)(2,1)S(1)} %copy-done.13, f32[576]{0:T(1024)S(1)} %fusion.48), kind=kOutput, calls=%fused_computation.33 | convolution fusion | flops 2721595392 | bytes 9144576 | tf_op jit(solution)/shard_map/dot_general | solution.py:102
  403.6 35.1 %reduce-scatter.14.cloned.1.call-done = bf16[192,2304]{1,0:T(8,128)(2,1)} async-done(((bf16[768,2304]{1,0:T(8,128)(2,1)}), bf16[192,2304]{1,0:T(8,128)(2,1)}) %reduce-scatter.14.cloned.1.call-update) | async-done | bytes 884752 | tf_op jit(solution)/shard_map/reduce_scatter | solution.py:156
  438.6 87.8 %reduce-scatter.18.cloned.1.call-done = bf16[192,3072]{1,0:T(8,128)(2,1)} async-done(((bf16[768,3072]{1,0:T(8,128)(2,1)}), bf16[192,3072]{1,0:T(8,128)(2,1)}) %reduce-scatter.18.cloned.1.call-update) | async-done | bytes 1179664 | tf_op jit(solution)/shard_map/reduce_scatter | solution.py:162
  526.4 88.1 %reduce-scatter.20.cloned.1.call-done = bf16[768,768]{1,0:T(8,128)(2,1)} async-done(((bf16[3072,768]{1,0:T(8,128)(2,1)}), bf16[768,768]{1,0:T(8,128)(2,1)}) %reduce-scatter.20.cloned.1.call-update) | async-done | bytes 1179664 | tf_op jit(solution)/shard_map/reduce_scatter | solution.py:165
  624.3 13.3 %reduce-scatter.22.cloned.1.call-done = bf16[192,2]{1,0:T(8,128)(2,1)} async-done(((bf16[768,2]{1,0:T(8,128)(2,1)}), bf16[192,2]{1,0:T(8,128)(2,1)}) %reduce-scatter.22.cloned.1.call-update) | async-done | bytes 784
  638.4 19.1 %reduce-scatter.24.cloned.1.call-done = bf16[192,2]{1,0:T(8,128)(2,1)} async-done(((bf16[768,2]{1,0:T(8,128)(2,1)}), bf16[192,2]{1,0:T(8,128)(2,1)}) %reduce-scatter.24.cloned.1.call-update) | async-done | bytes 784
  658.4 19.3 %reduce-scatter.26.cloned.1.call-done = bf16[192,2]{1,0:T(8,128)(2,1)} async-done(((bf16[768,2]{1,0:T(8,128)(2,1)}), bf16[192,2]{1,0:T(8,128)(2,1)}) %reduce-scatter.26.cloned.1.call-update) | async-done | bytes 784
  678.5 12.2 %all-reduce = (bf16[2,192]{1,0:T(2,128)(2,1)S(1)}, bf16[2,192]{1,0:T(2,128)(2,1)S(1)}, bf16[2,192]{1,0:T(2,128)(2,1)S(1)}) all-reduce(bf16[2,192]{1,0:T(2,128)(2,1)S(1)} %copy.84, bf16[2,192]{1,0:T(2,128)(2,1)S(1)} %copy.86, bf16[2,192]{1,0:T(2,128)(2,1)S(1)} %copy.88), channel_id=1, replica_groups=mesh['dp'=8,'fsdp'=4] {'dp'}, use_global_device_ids=true, to_apply=%region_32.33 | all-reduce | flops 1152 | bytes 4608 | tf_op jit(solution)/shard_map/psum | solution.py:183
  692.5 60.7 %all-reduce.4.cloned.1.call-done = (bf16[192,2304]{1,0:T(8,128)(2,1)}, bf16[192,768]{1,0:T(8,128)(2,1)}, bf16[192,3072]{1,0:T(8,128)(2,1)}, bf16[768,768]{1,0:T(8,128)(2,1)}) async-done(((bf16[192,2304]{1,0:T(8,128)(2,1)}, bf16[192,768]{1,0:T(8,128)(2,1)}, bf16[192,3072]{1,0:T(8,128)(2,1)}, bf16[768,768]{1,0:T(8,128)(2,1)}), (bf16[192,2304]{1,0:T(8,128)(2,1)}, bf16[192,768]{1,0:T(8,128)(2,1)}, ...) | async-done | bytes 3538960 | tf_op jit(solution)/shard_map/psum | solution.py:179
  (205 shorter events, 103.4 us)
Async XLA Ops:
  7.2 17.2 %copy-start.33 = (bf16[2,192]{1,0:T(2,128)(2,1)S(1)}, bf16[2,192]{1,0:T(2,128)(2,1)}, u32[]{:S(2)}) copy-start(bf16[2,192]{1,0:T(2,128)(2,1)} %param.17) | copy-start | bytes 2308
  7.2 25.3 %copy-start.34 = (bf16[2,192]{1,0:T(2,128)(2,1)S(1)}, bf16[2,192]{1,0:T(2,128)(2,1)}, u32[]{:S(2)}) copy-start(bf16[2,192]{1,0:T(2,128)(2,1)} %param.18) | copy-start | bytes 2308
  7.2 36.2 %copy-start.5 = (bf16[576,768]{1,0:T(8,128)(2,1)S(1)}, bf16[576,768]{1,0:T(8,128)(2,1)}, u32[]{:S(2)}) copy-start(bf16[576,768]{1,0:T(8,128)(2,1)} %param.10) | copy-start | bytes 2654212
  7.2 75.1 %all-gather.8.cloned.1.call-start = ((), (), s32[]{:S(2)}) async-start(), calls=%async_computation.7 | async-start | bytes 4423680 | tf_op jit(solution)/shard_map/all_gather | solution.py:33
  8.0 119.4 %all-gather.10.cloned.1.call-start = ((), (), s32[]{:S(2)}) async-start(), calls=%async_computation.8 | async-start | bytes 1474560 | tf_op jit(solution)/shard_map/all_gather | solution.py:34
  8.7 194.4 %all-gather.12.cloned.1.call-start = ((), (), s32[]{:S(2)}) async-start(), calls=%async_computation.9 | async-start | bytes 5898240 | tf_op jit(solution)/shard_map/all_gather | solution.py:35
  9.4 282.9 %all-gather.14.cloned.1.call-start = ((), (), s32[]{:S(2)}) async-start(), calls=%async_computation.10 | async-start | bytes 5898240 | tf_op jit(solution)/shard_map/all_gather | solution.py:36
  10.0 393.5 %reduce-scatter.16.cloned.1.call-start = ((), (), s32[]{:S(2)}) async-start(), calls=%async_computation.12 | async-start | bytes 1474560 | tf_op jit(solution)/shard_map/reduce_scatter | solution.py:159
  43.7 43.0 %copy-start.22 = (f32[576]{0:T(1024)}, f32[576]{0:T(1024)S(1)}, u32[]{:S(2)}) copy-start(f32[576]{0:T(1024)S(1)} %broadcast_multiply_fusion.5) | copy-start | bytes 6916
  44.1 42.6 %copy-start.24 = (f32[576]{0:T(1024)}, f32[576]{0:T(1024)S(1)}, u32[]{:S(2)}) copy-start(f32[576]{0:T(1024)S(1)} %fusion.28) | copy-start | bytes 6916
  44.1 42.6 %copy-start.28 = (f32[576]{0:T(1024)}, f32[576]{0:T(1024)S(1)}, u32[]{:S(2)}) copy-start(f32[576]{0:T(1024)S(1)} %fusion.49) | copy-start | bytes 6916
  44.5 42.2 %copy-start.26 = (f32[768]{0:T(1024)}, f32[768]{0:T(1024)S(1)}, u32[]{:S(2)}) copy-start(f32[768]{0:T(1024)S(1)} %get-tuple-element.101) | copy-start | bytes 9220
  44.5 42.2 %copy-start.30 = (f32[768]{0:T(1024)}, f32[768]{0:T(1024)S(1)}, u32[]{:S(2)}) copy-start(f32[768]{0:T(1024)S(1)} %get-tuple-element.74) | copy-start | bytes 9220
  312.4 126.3 %reduce-scatter.14.cloned.1.call-start = ((), (), s32[]{:S(2)}) async-start(), calls=%async_computation.11 | async-start | bytes 4423680 | tf_op jit(solution)/shard_map/reduce_scatter | solution.py:156
  318.2 19.6 %slice-start = ((s8[17694720]{0:T(1024)(128)(4,1)}), s8[4194304]{0:T(1024)(128)(4,1)S(1)}, s32[]{:S(2)}) async-start(s8[17694720]{0:T(1024)(128)(4,1)} %bitcast.91), calls=%async_computation.19 | async-start | bytes 8388608
  318.2 19.6 %slice-start.1 = ((s8[17694720]{0:T(1024)(128)(4,1)}), s8[917504]{0:T(1024)(128)(4,1)S(1)}, s32[]{:S(2)}) async-start(s8[17694720]{0:T(1024)(128)(4,1)} %bitcast.91), calls=%async_computation.20 | async-start | bytes 1835008
  325.8 12.5 %slice-start.4 = ((s8[17694720]{0:T(1024)(128)(4,1)}), s8[4194304]{0:T(1024)(128)(4,1)S(1)}, s32[]{:S(2)}) async-start(s8[17694720]{0:T(1024)(128)(4,1)} %bitcast.91), calls=%async_computation.23 | async-start | bytes 8388608
  373.5 152.9 %reduce-scatter.18.cloned.1.call-start = ((), (), s32[]{:S(2)}) async-start(), calls=%async_computation.13 | async-start | bytes 5898240 | tf_op jit(solution)/shard_map/reduce_scatter | solution.py:162
  382.7 231.8 %reduce-scatter.20.cloned.1.call-start = ((), (), s32[]{:S(2)}) async-start(), calls=%async_computation.14 | async-start | bytes 5898240 | tf_op jit(solution)/shard_map/reduce_scatter | solution.py:165
  391.9 245.7 %reduce-scatter.22.cloned.1.call-start = ((), (), s32[]{:S(2)}) async-start(), calls=%async_computation.15 | async-start | bytes 245760
  401.4 256.1 %reduce-scatter.24.cloned.1.call-start = ((), (), s32[]{:S(2)}) async-start(), calls=%async_computation.16 | async-start | bytes 245760
  402.5 275.1 %reduce-scatter.26.cloned.1.call-start = ((), (), s32[]{:S(2)}) async-start(), calls=%async_computation.17 | async-start | bytes 245760
  402.6 212.0 %copy-start.4 = (f32[576,768]{1,0:T(8,128)S(1)}, f32[576,768]{1,0:T(8,128)}, u32[]{:S(2)}) copy-start(f32[576,768]{1,0:T(8,128)} %copy-done.3) | copy-start | bytes 5308420
  403.5 349.7 %all-reduce.4.cloned.1.call-start = ((), (), s32[]{:S(2)}) async-start(), calls=%async_computation.18 | async-start | bytes 7077888 | tf_op jit(solution)/shard_map/psum | solution.py:179
  (33 other events, 163.3 us)
Sparse Core Ops, SparseCore 0:
  9.6 72.6 all-gather.7
  83.9 28.9 all-gather.9
  114.4 88.6 all-gather.11
  204.5 87.7 all-gather.13
  312.5 27.7 reduce-scatter.15
  373.6 64.9 reduce-scatter.13
  440.9 85.4 reduce-scatter.17
  528.7 85.7 reduce-scatter.19
  617.4 20.1 reduce-scatter.21
  639.7 17.8 reduce-scatter.23
  659.8 17.8 reduce-scatter.25
  681.2 71.9 all-reduce.3
where the time goes:
time: 772 us; the launch traced here: 768 us
  waiting for transfers between devices  502 us (65%)
  matrix products  126 us (16%)
  other arithmetic  52.6 us (7%)
  blocking collectives  43.7 us (6%)
  local copies, waits for them, and re-layouts  27.9 us (4%)
  between operations  15.2 us (2%)
    reduce_scatter x1, waiting for transfers between devices, on_device(): lax.psum_scatter(summands[3].astype(jnp.bfloat16), 'fsdp', scatter_dimens...  88.1 us
    reduce_scatter x1, waiting for transfers between devices, on_device(): lax.psum_scatter(summands[2].astype(jnp.bfloat16), 'fsdp', scatter_dimens...  87.8 us
    all_gather x1, waiting for transfers between devices, on_device(): lax.all_gather(w_up, 'fsdp', axis=0, tiled=True)  71.6 us
    all_gather x1, waiting for transfers between devices, on_device(): lax.all_gather(w_down, 'fsdp', axis=0, tiled=True)  66.5 us
    psum x1, waiting for transfers between devices, on_device(): lax.psum(pieces[0].astype(jnp.bfloat16), 'dp').astype(jnp.float32)  60.7 us
    unnamed x15, waiting for transfers between devices  54.3 us
    all_gather x1, waiting for transfers between devices, on_device(): lax.all_gather(w_qkv, 'fsdp', axis=0, tiled=True)  37.8 us
    reduce_scatter x1, waiting for transfers between devices, on_device(): lax.psum_scatter(summands[0].astype(jnp.bfloat16), 'fsdp', scatter_dimens...  35.1 us
  transfers between devices with their start and end apart: 12, of which 10 were waited for; matrix products, arithmetic and copies ran while one was open for 22% of the time, Pallas kernels for 0%

commit v1 on v0

--- a/solution.py
+++ b/solution.py
@@ -10,6 +10,28 @@
 epsilon = 1e-06
 
 
+def in_order(pieces, dim):
+    pieces = jnp.moveaxis(pieces, 0, dim)
+    shape = pieces.shape
+    return pieces.reshape(*shape[:dim], shape[dim] * shape[dim + 1], *shape[dim + 2 :])
+
+
+def grow_blocks(x, axis):
+    size = lax.axis_size(axis)
+    parts = x[None]
+    for level in range(size.bit_length() - 1):
+        bit = 1 << level
+        other = lax.ppermute(parts, axis, [(i, i ^ bit) for i in range(size)])
+        both = jnp.stack([parts, other])
+        upper = lax.axis_index(axis) >> level & 1
+        parts = jnp.where(upper == 0, both, both[::-1]).reshape(-1, *x.shape)
+    return parts
+
+
+def doubled_up(x, axis, dim):
+    return in_order(grow_blocks(x, axis), dim)
+
+
 def layer_norm(v, gain_row, bias_row):
     centre = v - jnp.mean(v, axis=-1, keepdims=True)
     spread = jnp.mean(centre * centre, axis=-1, keepdims=True)
@@ -30,7 +52,7 @@
     tokens, image_lengths, w_qkv, w_out, w_up, w_down, ln_gain, ln_bias, qk_gain, cotangent
 ):
     full_qkv, full_out, full_up, full_down, gain_all, bias_all, qk_all = (
-        lax.all_gather(w_qkv, "fsdp", axis=0, tiled=True),
+        doubled_up(w_qkv, "fsdp", 0),
         lax.all_gather(w_out, "fsdp", axis=0, tiled=True),
         lax.all_gather(w_up, "fsdp", axis=0, tiled=True),
         lax.all_gather(w_down, "fsdp", axis=0, tiled=True),

time: 772 us -> 806 us (1.044)
  blocking collectives: 43.7 us -> 74.5 us
    ppermute x0 -> x2, waiting for transfers between devices: none -> 138 us  [grow_blocks(): other = lax.ppermute(parts, axis, [(i, i ^ bit) for i in range(size)])]
    all_gather x1, waiting for transfers between devices: 71.6 us -> 0.02 us  [on_device(): lax.all_gather(w_up, 'fsdp', axis=0, tiled=True)]
    all_gather x1, waiting for transfers between devices: 66.5 us -> 10.4 us  [on_device(): lax.all_gather(w_down, 'fsdp', axis=0, tiled=True)]
    all_gather x1, waiting for transfers between devices: 37.8 us -> 0.01 us  [on_device(): lax.all_gather(w_qkv, 'fsdp', axis=0, tiled=True)]
    all_gather x1, blocking collectives: 12.7 us -> 43.9 us  [on_device(): lax.all_gather(ln_gain, 'fsdp', axis=1, tiled=True)]
    reduce_scatter x1, waiting for transfers between devices: 35.1 us -> 54.5 us  [on_device(): lax.psum_scatter(summands[0].astype(jnp.bfloat16), 'fsdp', scatter_dimens...]
  transfers between devices with their start and end apart: 12 -> 14, of which waited for: 10 -> 9; matrix products, arithmetic and copies ran while one was open for 22% -> 24% of each run, Pallas kernels for 0% -> 0%
where the time goes in v1:
time: 806 us; the launch traced here: 800 us
  waiting for transfers between devices  494 us (61%)
  matrix products  126 us (16%)
  blocking collectives  74.5 us (9%)
  other arithmetic  57.4 us (7%)
  local copies, waits for them, and re-layouts  28.1 us (3%)
  between operations  15.3 us (2%)
    ppermute x2, waiting for transfers between devices, grow_blocks(): other = lax.ppermute(parts, axis, [(i, i ^ bit) for i in range(size)])  138 us
    reduce_scatter x1, waiting for transfers between devices, on_device(): lax.psum_scatter(summands[3].astype(jnp.bfloat16), 'fsdp', scatter_dimens...  88.1 us
    reduce_scatter x1, waiting for transfers between devices, on_device(): lax.psum_scatter(summands[2].astype(jnp.bfloat16), 'fsdp', scatter_dimens...  87.8 us
    psum x1, waiting for transfers between devices, on_device(): lax.psum(pieces[0].astype(jnp.bfloat16), 'dp').astype(jnp.float32)  60.7 us
    reduce_scatter x1, waiting for transfers between devices, on_device(): lax.psum_scatter(summands[0].astype(jnp.bfloat16), 'fsdp', scatter_dimens...  54.5 us
    unnamed x15, waiting for transfers between devices  54.4 us
    all_gather x1, blocking collectives, on_device(): lax.all_gather(ln_gain, 'fsdp', axis=1, tiled=True)  43.9 us
    dot_general x1, matrix products, on_device(): up_pre = jnp.dot(second_low, full_up, preferred_element_type=jnp.float32)  22.7 us
  transfers between devices with their start and end apart: 14, of which 9 were waited for; matrix products, arithmetic and copies ran while one was open for 24% of the time, Pallas kernels for 0%

profile of v1, /device:TPU:0, one launch (start us, length us, event | category | flops | bytes accessed | tf_op | source)
XLA Modules:
  0.0 799.8 jit_solution(17368369612413821291)
XLA Ops:
  12.7 43.9 %all-gather = bf16[4,192,2]{1,2,0:T(2,128)(2,1)S(1)} all-gather(bf16[1,192,2]{1,2,0:T(2,128)(2,1)S(1)} %bitcast.140), channel_id=1, replica_groups=mesh['dp'=8,'fsdp'=4] {'fsdp'}, dimensions={0}, use_global_device_ids=true | all-gather | bytes 3840 | tf_op jit(solution)/shard_map/all_gather | solution.py:59
  56.7 7.6 all-gather.1
  64.4 10.8 %all-gather.2 = bf16[4,192,2]{1,2,0:T(2,128)(2,1)S(1)} all-gather(bf16[1,192,2]{1,2,0:T(2,128)(2,1)S(1)} %bitcast.142), channel_id=1, replica_groups=mesh['dp'=8,'fsdp'=4] {'fsdp'}, dimensions={0}, use_global_device_ids=true | all-gather | bytes 3840 | tf_op jit(solution)/shard_map/all_gather | solution.py:61
  80.4 137.7 %collective-permute-done.1 = bf16[2,192,2304]{2,1,0:T(8,128)(2,1)S(1)} collective-permute-done((bf16[2,192,2304]{2,1,0:T(8,128)(2,1)S(1)}, bf16[2,192,2304]{2,1,0:T(8,128)(2,1)S(1)}, u32[]{:S(2)}, u32[]{:S(2)}) %collective-permute-start.1) | collective-permute-done | bytes 1769504 | tf_op jit(solution)/shard_map/ppermute | solution.py:24
  235.7 11.3 %fusion.64 = (f32[12,576]{1,0:T(8,128)S(1)}, f32[12,576,576]{1,2,0:T(8,128)}) fusion(f32[576,12,64]{0,2,1:T(8,128)S(1)} %bitcast.104, f32[12,64]{1,0:T(8,128)S(1)} %mul.324, f32[576,12]{0,1:T(8,128)S(1)} %get-tuple-element.104, f32[576,12]{0,1:T(8,128)S(1)} %broadcast_multiply_fusion, f32[576,12,64]{0,2,1:T(8,128)} %bitcast.111, f32[12,64]{1,0:T(8,128)S(1)} %mul.318, ...), kind=kOutput, calls=%fused_computation.145 | convolution fusion | flops 525083904 | bytes 19940352 | tf_op jit(solution)/shard_map/while/body/eval_jaxpr/qhd,khd->hqk/dot_general | solution.py:89
  246.9 8.6 %fusion.3 = f32[12,576]{1,0:T(8,128)S(1)} fusion(f32[12,576,576]{1,2,0:T(8,128)} %get-tuple-element.93, f32[12,576]{1,0:T(8,128)S(1)} %get-tuple-element.92), kind=kLoop, calls=%fused_computation.9 | loop fusion | flops 7955712 | bytes 15980544 | tf_op jit(solution)/shard_map/while/body/eval_jaxpr/reduce_sum | solution.py:99
  255.6 10.7 %fusion.31 = bf16[12,64,576]{2,1,0:T(8,128)(2,1)} fusion(bf16[576,12,64]{0,2,1:T(8,128)(2,1)} %bitcast.118, f32[12,576,576]{1,2,0:T(8,128)} %get-tuple-element.93, f32[12,576]{1,0:T(8,128)S(1)} %fusion.3, f32[12,576]{1,0:T(8,128)S(1)} %get-tuple-element.92), kind=kOutput, calls=%fused_computation.85 | convolution fusion | flops 521994240 | bytes 17750016 | tf_op jit(solution)/shard_map/while/body/eval_jaxpr/hqk,khd->qhd/dot_general | solution.py:101
  270.4 22.7 %multiply_convert_fusion = (bf16[576,3072]{1,0:T(8,128)(2,1)}, f32[576,3072]{1,0:T(8,128)}, f32[576,3072]{1,0:T(8,128)}) fusion(bf16[768,3072]{1,0:T(8,128)(2,1)} %all-gather.10.cloned.1.call-done, f32[576,768]{1,0:T(8,128)} %copy-done.7, f32[768]{0:T(1024)S(1)} %get-tuple-element.73, f32[768]{0:T(1024)S(1)} %get-tuple-element.71, f32[576]{0:T(1024)S(1)} %fusion.52, ...), kind=kOutput, calls=%fused_computation.17 | convolution fusion | flops 2835136512 | bytes 24193536 | tf_op jit(solution)/shard_map/dot_general | solution.py:111
  293.1 10.4 %all-gather.12.cloned.1.call-done = bf16[3072,768]{1,0:T(8,128)(2,1)} async-done(((bf16[768,768]{1,0:T(8,128)(2,1)}), bf16[3072,768]{1,0:T(8,128)(2,1)}) %all-gather.12.cloned.1.call-update) | async-done | bytes 4718608 | tf_op jit(solution)/shard_map/all_gather | solution.py:58
  303.5 11.5 %add_convert_fusion = bf16[576,3072]{1,0:T(8,128)(2,1)S(1)} fusion(f32[576,3072]{1,0:T(8,128)} %get-tuple-element.87, f32[576,3072]{1,0:T(8,128)} %get-tuple-element.96, bf16[3072,768]{1,0:T(8,128)(2,1)} %all-gather.12.cloned.1.call-done, bf16[576,768]{1,0:T(8,128)(2,1)} %param.19, f32[576]{0:T(1024)S(1)} %fusion.50), kind=kOutput, calls=%fused_computation.16 | convolution fusion | flops 2744008704 | bytes 23300352 | tf_op jit(solution)/shard_map/dot_general | solution.py:125
  325.7 7.6 convolution_convert_fusion
  333.3 12.0 %fusion = f32[12,576]{1,0:T(8,128)S(1)} fusion(bf16[12,576,576]{1,2,0:T(8,128)(2,1)} %convolution_convert_fusion, f32[12,576,576]{1,2,0:T(8,128)} %get-tuple-element.93, f32[12,576]{1,0:T(8,128)S(1)} %log_add_fusion), kind=kLoop, calls=%fused_computation.2 | loop fusion | flops 15918336 | bytes 23943168 | tf_op jit(solution)/shard_map/while/body/eval_jaxpr/reduce_sum | solution.py:145
  370.7 9.1 %fusion.32 = bf16[12,64,576]{2,1,0:T(8,128)(2,1)S(1)} fusion(bf16[576,12,64]{0,2,1:T(8,128)(2,1)S(1)} %bitcast.117, f32[12,576,576]{1,2,0:T(8,128)} %get-tuple-element.93, f32[12,576]{1,0:T(8,128)S(1)} %log_add_fusion), kind=kOutput, calls=%fused_computation.86 | convolution fusion | flops 518012928 | bytes 17722368 | tf_op jit(solution)/shard_map/while/body/eval_jaxpr/hqk,qhd->khd/dot_general | solution.py:142
  380.8 7.2 convolution_convert_fusion.1
  389.5 7.8 convolution_convert_fusion.3
  398.4 8.0 %convolution_convert_fusion.2 = bf16[3072,768]{1,0:T(8,128)(2,1)} fusion(bf16[576,3072]{1,0:T(8,128)(2,1)} %get-tuple-element.86, bf16[576,768]{1,0:T(8,128)(2,1)S(1)} %copy-done.15, f32[576]{0:T(1024)S(1)} %fusion.50), kind=kOutput, calls=%fused_computation.34 | convolution fusion | flops 2721595392 | bytes 9144576 | tf_op jit(solution)/shard_map/dot_general | solution.py:124
  416.3 54.5 %reduce-scatter.14.cloned.1.call-done = bf16[192,2304]{1,0:T(8,128)(2,1)} async-done(((bf16[768,2304]{1,0:T(8,128)(2,1)}), bf16[192,2304]{1,0:T(8,128)(2,1)}) %reduce-scatter.14.cloned.1.call-update) | async-done | bytes 884752 | tf_op jit(solution)/shard_map/reduce_scatter | solution.py:178
  470.8 87.8 %reduce-scatter.18.cloned.1.call-done = bf16[192,3072]{1,0:T(8,128)(2,1)} async-done(((bf16[768,3072]{1,0:T(8,128)(2,1)}), bf16[192,3072]{1,0:T(8,128)(2,1)}) %reduce-scatter.18.cloned.1.call-update) | async-done | bytes 1179664 | tf_op jit(solution)/shard_map/reduce_scatter | solution.py:184
  558.5 88.1 %reduce-scatter.20.cloned.1.call-done = bf16[768,768]{1,0:T(8,128)(2,1)} async-done(((bf16[3072,768]{1,0:T(8,128)(2,1)}), bf16[768,768]{1,0:T(8,128)(2,1)}) %reduce-scatter.20.cloned.1.call-update) | async-done | bytes 1179664 | tf_op jit(solution)/shard_map/reduce_scatter | solution.py:187
  656.4 12.7 %reduce-scatter.26.cloned.1.call-done = bf16[192,2]{1,0:T(8,128)(2,1)} async-done(((bf16[768,2]{1,0:T(8,128)(2,1)}), bf16[192,2]{1,0:T(8,128)(2,1)}) %reduce-scatter.26.cloned.1.call-update) | async-done | bytes 784
  670.0 19.7 %reduce-scatter.24.cloned.1.call-done = bf16[192,2]{1,0:T(8,128)(2,1)} async-done(((bf16[768,2]{1,0:T(8,128)(2,1)}), bf16[192,2]{1,0:T(8,128)(2,1)}) %reduce-scatter.24.cloned.1.call-update) | async-done | bytes 784
  690.5 19.8 %reduce-scatter.22.cloned.1.call-done = bf16[192,2]{1,0:T(8,128)(2,1)} async-done(((bf16[768,2]{1,0:T(8,128)(2,1)}), bf16[192,2]{1,0:T(8,128)(2,1)}) %reduce-scatter.22.cloned.1.call-update) | async-done | bytes 784
  711.2 12.2 %all-reduce = (bf16[2,192]{1,0:T(2,128)(2,1)S(1)}, bf16[2,192]{1,0:T(2,128)(2,1)S(1)}, bf16[2,192]{1,0:T(2,128)(2,1)S(1)}) all-reduce(bf16[2,192]{1,0:T(2,128)(2,1)S(1)} %copy.84, bf16[2,192]{1,0:T(2,128)(2,1)S(1)} %copy.86, bf16[2,192]{1,0:T(2,128)(2,1)S(1)} %copy.88), channel_id=1, replica_groups=mesh['dp'=8,'fsdp'=4] {'dp'}, use_global_device_ids=true, to_apply=%region_32.33 | all-reduce | flops 1152 | bytes 4608 | tf_op jit(solution)/shard_map/psum | solution.py:205
  725.2 60.7 %all-reduce.4.cloned.1.call-done = (bf16[192,2304]{1,0:T(8,128)(2,1)}, bf16[192,768]{1,0:T(8,128)(2,1)}, bf16[192,3072]{1,0:T(8,128)(2,1)}, bf16[768,768]{1,0:T(8,128)(2,1)}) async-done(((bf16[192,2304]{1,0:T(8,128)(2,1)}, bf16[192,768]{1,0:T(8,128)(2,1)}, bf16[192,3072]{1,0:T(8,128)(2,1)}, bf16[768,768]{1,0:T(8,128)(2,1)}), (bf16[192,2304]{1,0:T(8,128)(2,1)}, bf16[192,768]{1,0:T(8,128)(2,1)}, ...) | async-done | bytes 3538960 | tf_op jit(solution)/shard_map/psum | solution.py:201
  (221 shorter events, 102.1 us)
Async XLA Ops:
  7.2 69.1 %copy-start.13 = (bf16[192,2304]{1,0:T(8,128)(2,1)S(1)}, bf16[192,2304]{1,0:T(8,128)(2,1)}, u32[]{:S(2)}) copy-start(bf16[192,2304]{1,0:T(8,128)(2,1)} %param.12) | copy-start | bytes 2654212
  7.2 49.5 %copy-start.36 = (bf16[2,192]{1,0:T(2,128)(2,1)S(1)}, bf16[2,192]{1,0:T(2,128)(2,1)}, u32[]{:S(2)}) copy-start(bf16[2,192]{1,0:T(2,128)(2,1)} %param.17) | copy-start | bytes 2308
  7.2 57.2 %copy-start.37 = (bf16[2,192]{1,0:T(2,128)(2,1)S(1)}, bf16[2,192]{1,0:T(2,128)(2,1)}, u32[]{:S(2)}) copy-start(bf16[2,192]{1,0:T(2,128)(2,1)} %param.18) | copy-start | bytes 2308
  7.2 68.2 %copy-start.40 = (s32[1,9]{1,0:T(1,128)S(1)}, s32[1,9]{1,0:T(1,128)}, u32[]{:S(2)}) copy-start(s32[1,9]{1,0:T(1,128)} %param.11) | copy-start | bytes 112
  7.2 259.0 %all-gather.8.cloned.1.call-start = ((), (), s32[]{:S(2)}) async-start(), calls=%async_computation.7 | async-start | bytes 1474560 | tf_op jit(solution)/shard_map/all_gather | solution.py:56
  8.0 262.4 %all-gather.10.cloned.1.call-start = ((), (), s32[]{:S(2)}) async-start(), calls=%async_computation.8 | async-start | bytes 5898240 | tf_op jit(solution)/shard_map/all_gather | solution.py:57
  8.7 294.8 %all-gather.12.cloned.1.call-start = ((), (), s32[]{:S(2)}) async-start(), calls=%async_computation.9 | async-start | bytes 5898240 | tf_op jit(solution)/shard_map/all_gather | solution.py:58
  9.5 398.1 %all-gather.14.cloned.1.call-start = ((), (), s32[]{:S(2)}) async-start(), calls=%async_computation.10 | async-start | bytes 4423680 | tf_op jit(solution)/shard_map/all_gather | solution.py:117
  9.5 66.8 %collective-permute-start = (bf16[1,192,2304]{2,1,0:T(8,128)(2,1)S(1)}, bf16[1,192,2304]{2,1,0:T(8,128)(2,1)S(1)}, u32[]{:S(2)}, u32[]{:S(2)}) collective-permute-start(bf16[1,192,2304]{2,1,0:T(8,128)(2,1)S(1)} %bitcast.121), channel_id=1, source_target_pairs={{0,1},{1,0},{2,3},{3,2},{4,5},{5,4},{6,7},{7,6},{8,9},{9,8},{10,11... | collective-permute-start | bytes 2654216 | tf_op jit(solution)/shard_map/ppermute | solution.py:24
  12.7 403.7 %reduce-scatter.16.cloned.1.call-start = ((), (), s32[]{:S(2)}) async-start(), calls=%async_computation.12 | async-start | bytes 1474560 | tf_op jit(solution)/shard_map/reduce_scatter | solution.py:181
  76.3 142.8 %copy-start.29 = (f32[768]{0:T(1024)}, f32[768]{0:T(1024)S(1)}, u32[]{:S(2)}) copy-start(f32[768]{0:T(1024)S(1)} %get-tuple-element.72) | copy-start | bytes 9220
  76.8 141.3 %collective-permute-start.1 = (bf16[2,192,2304]{2,1,0:T(8,128)(2,1)S(1)}, bf16[2,192,2304]{2,1,0:T(8,128)(2,1)S(1)}, u32[]{:S(2)}, u32[]{:S(2)}) collective-permute-start(bf16[2,192,2304]{2,1,0:T(8,128)(2,1)S(1)} %get-tuple-element.91), channel_id=1, source_target_pairs={{0,2},{1,3},{2,0},{3,1},{4,6},{5,7},{6,4},{7,5},{8,10},{9,11},{10,... | collective-permute-start | bytes 5308424 | tf_op jit(solution)/shard_map/ppermute | solution.py:24
  78.7 140.4 %copy-start.33 = (f32[768]{0:T(1024)}, f32[768]{0:T(1024)S(1)}, u32[]{:S(2)}) copy-start(f32[768]{0:T(1024)S(1)} %get-tuple-element.74) | copy-start | bytes 9220
  79.0 140.1 %copy-start.25 = (f32[576]{0:T(1024)}, f32[576]{0:T(1024)S(1)}, u32[]{:S(2)}) copy-start(f32[576]{0:T(1024)S(1)} %broadcast_multiply_fusion.5) | copy-start | bytes 6916
  79.4 139.0 %copy-start.27 = (f32[576]{0:T(1024)}, f32[576]{0:T(1024)S(1)}, u32[]{:S(2)}) copy-start(f32[576]{0:T(1024)S(1)} %fusion.28) | copy-start | bytes 6916
  79.5 139.7 %copy-start.31 = (f32[576]{0:T(1024)}, f32[576]{0:T(1024)S(1)}, u32[]{:S(2)}) copy-start(f32[576]{0:T(1024)S(1)} %fusion.51) | copy-start | bytes 6916
  366.0 104.8 %reduce-scatter.14.cloned.1.call-start = ((), (), s32[]{:S(2)}) async-start(), calls=%async_computation.11 | async-start | bytes 4423680 | tf_op jit(solution)/shard_map/reduce_scatter | solution.py:178
  388.0 170.5 %reduce-scatter.18.cloned.1.call-start = ((), (), s32[]{:S(2)}) async-start(), calls=%async_computation.13 | async-start | bytes 5898240 | tf_op jit(solution)/shard_map/reduce_scatter | solution.py:184
  397.3 249.4 %reduce-scatter.20.cloned.1.call-start = ((), (), s32[]{:S(2)}) async-start(), calls=%async_computation.14 | async-start | bytes 5898240 | tf_op jit(solution)/shard_map/reduce_scatter | solution.py:187
  406.5 262.6 %reduce-scatter.26.cloned.1.call-start = ((), (), s32[]{:S(2)}) async-start(), calls=%async_computation.17 | async-start | bytes 245760
  413.5 276.2 %reduce-scatter.24.cloned.1.call-start = ((), (), s32[]{:S(2)}) async-start(), calls=%async_computation.16 | async-start | bytes 245760
  415.3 295.1 %reduce-scatter.22.cloned.1.call-start = ((), (), s32[]{:S(2)}) async-start(), calls=%async_computation.15 | async-start | bytes 245760
  415.4 231.4 %copy-start.4 = (f32[576,768]{1,0:T(8,128)S(1)}, f32[576,768]{1,0:T(8,128)}, u32[]{:S(2)}) copy-start(f32[576,768]{1,0:T(8,128)} %copy-done.3) | copy-start | bytes 5308420
  416.2 369.6 %all-reduce.4.cloned.1.call-start = ((), (), s32[]{:S(2)}) async-start(), calls=%async_computation.18 | async-start | bytes 7077888 | tf_op jit(solution)/shard_map/psum | solution.py:201
  (39 other events, 226.8 us)
Sparse Core Ops, SparseCore 0:
  9.6 41.5 all-gather.7
  52.8 161.4 all-gather.9
  215.9 87.5 all-gather.11
  304.9 68.3 all-gather.13
  375.5 27.9 reduce-scatter.15
  405.6 65.1 reduce-scatter.13
  473.1 85.4 reduce-scatter.17
  560.8 85.7 reduce-scatter.19
  649.0 20.1 reduce-scatter.25
  671.8 17.8 reduce-scatter.23
  692.5 17.8 reduce-scatter.21
  713.9 71.9 all-reduce.3
